TPU v7x, 32 devices: a whole 2x2x4 slice. The times are simulated.
32 devices in a mesh: chain: 8 (over z, x), grp: 4 (over y, core).
Axes of the slice: x: 2, y: 2, z: 4, core: 2. Of those that a mesh axis runs over, the one named last changes fastest.
Arguments:
- right_side: float32 [16, 4, 64, 128], P('chain', 'grp'), may hold values from -0.8 to 0.8
- factor: float32 [16, 4, 2, 128, 128], P('chain', 'grp'), may hold values from -1 to 1
- inverse_diag: float32 [16, 4, 128, 128], P('chain', 'grp'), as said below
- pattern: int32 [16, 4, 2], P('chain'), may hold values from 0 to 3, as said below
Outputs:
- forward_result: float32 [16, 4, 64, 128], P('chain', 'grp')
- solution: float32 [16, 4, 64, 128], P('chain', 'grp')
Inputs may be any that keep to these rules, and one draw needn't show every extreme that they name: `pattern`: the 2 entries of one supernode are different supernodes of the previous level. `inverse_diag`: every block is lower triangular with a diagonal between 0.75 and 1.05.
All inputs are finite; a program needn't handle non-finite values.
Results may differ from a plain program's by a relative error of at most 0.0002.
Values sent between devices are 32-bit elements; how exact they have to be, the bound alone decides.
No kernel may reach another device: no remote copies, remote signals or barrier semaphores. Data moves between devices by JAX's collectives and lax.ppermute only.
A program may use at most 320 MiB of HBM per device.

v0:
```python
import jax
import jax.numpy as jnp
from jax import lax
from jax.sharding import PartitionSpec as P

PRECISE = lax.Precision.HIGHEST


def matmul(left_side, right_factor):
    return jnp.dot(left_side, right_factor, precision=PRECISE, preferred_element_type=jnp.float32)


def matmul_trans(left_side, right_factor):
    return lax.dot_general(
        left_side,
        right_factor,
        (((1,), (1,)), ((), ())),
        precision=PRECISE,
        preferred_element_type=jnp.float32,
    )


def shards(right_side, factor, inverse_diag, pattern):
    levels = right_side.shape[0]
    samples = right_side.shape[2]
    sup_rows = right_side.shape[3]
    groups = lax.axis_size("grp")
    chain = lax.axis_size("chain")
    level_rows = groups * sup_rows
    my_group = lax.axis_index("grp")
    scaled = jnp.einsum(
        "lgti,lgkij->lgktj",
        inverse_diag,
        factor,
        precision=PRECISE,
        preferred_element_type=jnp.float32,
    )
    lifted = jnp.einsum(
        "lgsi,lgti->lgst",
        right_side,
        inverse_diag,
        precision=PRECISE,
        preferred_element_type=jnp.float32,
    )
    blocks, offsets = (
        lax.all_gather(scaled, "grp", axis=1, tiled=True),
        lax.all_gather(lifted, "grp", axis=1, tiled=True),
    )
    onehot = (pattern[..., None] == jnp.arange(groups, dtype=jnp.int32)).astype(jnp.float32)
    level_maps = -jnp.einsum(
        "lgkh,lgktj->lhjgt", onehot, blocks, precision=PRECISE, preferred_element_type=jnp.float32
    )
    level_maps = level_maps.reshape(levels, level_rows, level_rows)
    sources = offsets.transpose(0, 2, 1, 3).reshape(levels, samples, level_rows)

    def forward_levels(state):
        rows = []
        for level in range(levels):
            state = matmul(state, level_maps[level]) + sources[level]
            rows.append(state)
        return rows

    ahead = [(position, position + 1) for position in range(chain - 1)]
    behind = [(position + 1, position) for position in range(chain - 1)]

    def forward_hop(_, state):
        return lax.ppermute(forward_levels(state)[-1], "chain", ahead)

    incoming = jnp.zeros((samples, level_rows), jnp.float32)
    incoming = lax.fori_loop(0, chain - 1, forward_hop, incoming)
    solved = forward_levels(incoming)

    def backward_levels(running):
        rows = [None] * levels
        for level in reversed(range(levels)):
            rows[level] = solved[level] - running
            running = matmul_trans(-rows[level], level_maps[level])
        return (rows, running)

    def backward_hop(_, running):
        return lax.ppermute(backward_levels(running)[1], "chain", behind)

    arriving = jnp.zeros((samples, level_rows), jnp.float32)
    arriving = lax.fori_loop(0, chain - 1, backward_hop, arriving)
    pending_rows, _ = backward_levels(arriving)
    forward_own = []
    answers = []
    for level in range(levels):
        forward_own.append(
            lax.dynamic_slice_in_dim(solved[level], my_group * sup_rows, sup_rows, 1)
        )
        own_rows = lax.dynamic_slice_in_dim(pending_rows[level], my_group * sup_rows, sup_rows, 1)
        answers.append(matmul(own_rows, inverse_diag[level, 0]))
    forward_own = jnp.stack(forward_own)
    answers = jnp.stack(answers)
    return (forward_own[:, None], answers[:, None])


def solution(mesh):
    return jax.shard_map(
        shards,
        mesh=mesh,
        in_specs=(
            P("chain", "grp", None, None),
            P("chain", "grp", None, None, None),
            P("chain", "grp", None, None),
            P("chain", None, None),
        ),
        out_specs=(P("chain", "grp", None, None), P("chain", "grp", None, None)),
        check_vma=False,
    )
```

profile of v0, /device:TPU:0, one launch (start us, length us, event | category | flops | bytes accessed | tf_op | source)
XLA Modules:
  0.0 224.4 jit_solution(18291246836347683198)
XLA Ops:
  8.1 1.5 convolution_bitcast_fusion
  11.3 1.3 fusion.22
  12.6 7.3 %all-gather = f32[2,256,128]{2,1,0:T(8,128)S(1)} all-gather(f32[2,64,128]{2,1,0:T(8,128)S(1)} %fusion.22), channel_id=2, replica_groups=mesh['chain'=8,'grp'=4] {'grp'}, dimensions={1}, use_global_device_ids=true | all-gather | bytes 327680 | tf_op jit(solution)/shard_map/all_gather | solution.py:47
  22.1 8.0 %all-gather.3.cloned.1.call-done = f32[2,4,2,128,128]{4,3,2,0,1:T(8,128)} async-done(((f32[2,1,2,128,128]{4,3,2,0,1:T(8,128)}), f32[2,4,2,128,128]{4,3,2,0,1:T(8,128)}) %all-gather.3.cloned.1.call-update) | async-done | bytes 1048592 | tf_op jit(solution)/shard_map/all_gather | solution.py:46
  30.1 3.9 %negate_bitcast_fusion = f32[2,4,128,4,128]{2,1,4,3,0:T(4,128)S(1)} fusion(f32[2,4,2,128,128]{4,3,2,0,1:T(8,128)} %all-gather.3.cloned.1.call-done, s32[2,4,2]{2,1,0:T(4,128)S(1)} %copy.17), kind=kOutput, calls=%fused_computation.15 | convolution fusion | flops 13107264 | bytes 3145792 | tf_op jit(solution)/shard_map/lgkh,lgktj->lhjgt/dot_general | solution.py:50
  34.0 1.9 reshape.33
  37.0 1.9 copy.20
  38.9 80.6 %while.20 = (s32[]{:T(128)}, f32[64,512]{1,0:T(8,128)S(1)}, f32[2,512,512]{2,1,0:T(8,128)S(1)}, f32[2,64,512]{2,1,0:T(8,128)}, s32[]{:T(128)}) while((s32[]{:T(128)}, f32[64,512]{1,0:T(8,128)S(1)}, f32[2,512,512]{2,1,0:T(8,128)S(1)}, f32[2,64,512]{2,1,0:T(8,128)}, s32[]{:T(128)}) %tuple.53), condition=%wide.region_1.0_spmd, body=%wide.region_0.0_spmd.sunk | while | flops 402718720 | bytes 3407973 | solution.py:70
  38.9 1.7 convolution_add_fusion.6
  40.6 2.3 %convolution_add_fusion.7 = f32[64,512]{1,0:T(8,128)} fusion(f32[64,512]{1,0:T(8,128)S(1)} %convolution_add_fusion.6, f32[2,512,512]{2,1,0:T(8,128)S(1)} %get-tuple-element.167, f32[2,64,512]{2,1,0:T(8,128)} %get-tuple-element.168), kind=kOutput, calls=%fused_computation.clone.1 | convolution fusion | flops 201359360 | bytes 1441792 | tf_op jit(solution)/shard_map/while/body/eval_jaxpr/dot_general | solution.py:10
  42.9 3.4 %collective-permute-start = (f32[64,512]{1,0:T(8,128)}, f32[64,512]{1,0:T(8,128)S(1)}, u32[]{:S(2)}, u32[]{:S(2)}) collective-permute-start(f32[64,512]{1,0:T(8,128)} %convolution_add_fusion.7), channel_id=1, source_target_pairs={{0,4},{4,8},{8,12},{12,16},{16,20},{20,24},{24,28},{1,5},{5,9},{9,... | collective-permute-start | bytes 393224 | tf_op jit(solution)/shard_map/while/body/eval_jaxpr/ppermute | solution.py:67
  46.3 3.4 %collective-permute-done = f32[64,512]{1,0:T(8,128)S(1)} collective-permute-done((f32[64,512]{1,0:T(8,128)}, f32[64,512]{1,0:T(8,128)S(1)}, u32[]{:S(2)}, u32[]{:S(2)}) %collective-permute-start) | collective-permute-done | bytes 131104 | tf_op jit(solution)/shard_map/while/body/eval_jaxpr/ppermute | solution.py:67
  49.7 1.7 convolution_add_fusion.6
  51.4 2.3 %convolution_add_fusion.7 = f32[64,512]{1,0:T(8,128)} fusion(f32[64,512]{1,0:T(8,128)S(1)} %convolution_add_fusion.6, f32[2,512,512]{2,1,0:T(8,128)S(1)} %get-tuple-element.167, f32[2,64,512]{2,1,0:T(8,128)} %get-tuple-element.168), kind=kOutput, calls=%fused_computation.clone.1 | convolution fusion | flops 201359360 | bytes 1441792 | tf_op jit(solution)/shard_map/while/body/eval_jaxpr/dot_general | solution.py:10
  53.7 4.3 %collective-permute-start = (f32[64,512]{1,0:T(8,128)}, f32[64,512]{1,0:T(8,128)S(1)}, u32[]{:S(2)}, u32[]{:S(2)}) collective-permute-start(f32[64,512]{1,0:T(8,128)} %convolution_add_fusion.7), channel_id=1, source_target_pairs={{0,4},{4,8},{8,12},{12,16},{16,20},{20,24},{24,28},{1,5},{5,9},{9,... | collective-permute-start | bytes 393224 | tf_op jit(solution)/shard_map/while/body/eval_jaxpr/ppermute | solution.py:67
  57.9 2.8 %collective-permute-done = f32[64,512]{1,0:T(8,128)S(1)} collective-permute-done((f32[64,512]{1,0:T(8,128)}, f32[64,512]{1,0:T(8,128)S(1)}, u32[]{:S(2)}, u32[]{:S(2)}) %collective-permute-start) | collective-permute-done | bytes 131104 | tf_op jit(solution)/shard_map/while/body/eval_jaxpr/ppermute | solution.py:67
  60.8 1.7 convolution_add_fusion.6
  62.4 2.3 %convolution_add_fusion.7 = f32[64,512]{1,0:T(8,128)} fusion(f32[64,512]{1,0:T(8,128)S(1)} %convolution_add_fusion.6, f32[2,512,512]{2,1,0:T(8,128)S(1)} %get-tuple-element.167, f32[2,64,512]{2,1,0:T(8,128)} %get-tuple-element.168), kind=kOutput, calls=%fused_computation.clone.1 | convolution fusion | flops 201359360 | bytes 1441792 | tf_op jit(solution)/shard_map/while/body/eval_jaxpr/dot_general | solution.py:10
  64.7 4.3 %collective-permute-start = (f32[64,512]{1,0:T(8,128)}, f32[64,512]{1,0:T(8,128)S(1)}, u32[]{:S(2)}, u32[]{:S(2)}) collective-permute-start(f32[64,512]{1,0:T(8,128)} %convolution_add_fusion.7), channel_id=1, source_target_pairs={{0,4},{4,8},{8,12},{12,16},{16,20},{20,24},{24,28},{1,5},{5,9},{9,... | collective-permute-start | bytes 393224 | tf_op jit(solution)/shard_map/while/body/eval_jaxpr/ppermute | solution.py:67
  69.0 2.8 %collective-permute-done = f32[64,512]{1,0:T(8,128)S(1)} collective-permute-done((f32[64,512]{1,0:T(8,128)}, f32[64,512]{1,0:T(8,128)S(1)}, u32[]{:S(2)}, u32[]{:S(2)}) %collective-permute-start) | collective-permute-done | bytes 131104 | tf_op jit(solution)/shard_map/while/body/eval_jaxpr/ppermute | solution.py:67
  71.8 1.7 convolution_add_fusion.6
  73.5 2.3 %convolution_add_fusion.7 = f32[64,512]{1,0:T(8,128)} fusion(f32[64,512]{1,0:T(8,128)S(1)} %convolution_add_fusion.6, f32[2,512,512]{2,1,0:T(8,128)S(1)} %get-tuple-element.167, f32[2,64,512]{2,1,0:T(8,128)} %get-tuple-element.168), kind=kOutput, calls=%fused_computation.clone.1 | convolution fusion | flops 201359360 | bytes 1441792 | tf_op jit(solution)/shard_map/while/body/eval_jaxpr/dot_general | solution.py:10
  75.8 5.1 %collective-permute-start = (f32[64,512]{1,0:T(8,128)}, f32[64,512]{1,0:T(8,128)S(1)}, u32[]{:S(2)}, u32[]{:S(2)}) collective-permute-start(f32[64,512]{1,0:T(8,128)} %convolution_add_fusion.7), channel_id=1, source_target_pairs={{0,4},{4,8},{8,12},{12,16},{16,20},{20,24},{24,28},{1,5},{5,9},{9,... | collective-permute-start | bytes 393224 | tf_op jit(solution)/shard_map/while/body/eval_jaxpr/ppermute | solution.py:67
  80.9 2.8 %collective-permute-done = f32[64,512]{1,0:T(8,128)S(1)} collective-permute-done((f32[64,512]{1,0:T(8,128)}, f32[64,512]{1,0:T(8,128)S(1)}, u32[]{:S(2)}, u32[]{:S(2)}) %collective-permute-start) | collective-permute-done | bytes 131104 | tf_op jit(solution)/shard_map/while/body/eval_jaxpr/ppermute | solution.py:67
  83.7 1.7 convolution_add_fusion.6
  85.4 2.3 %convolution_add_fusion.7 = f32[64,512]{1,0:T(8,128)} fusion(f32[64,512]{1,0:T(8,128)S(1)} %convolution_add_fusion.6, f32[2,512,512]{2,1,0:T(8,128)S(1)} %get-tuple-element.167, f32[2,64,512]{2,1,0:T(8,128)} %get-tuple-element.168), kind=kOutput, calls=%fused_computation.clone.1 | convolution fusion | flops 201359360 | bytes 1441792 | tf_op jit(solution)/shard_map/while/body/eval_jaxpr/dot_general | solution.py:10
  87.7 5.1 %collective-permute-start = (f32[64,512]{1,0:T(8,128)}, f32[64,512]{1,0:T(8,128)S(1)}, u32[]{:S(2)}, u32[]{:S(2)}) collective-permute-start(f32[64,512]{1,0:T(8,128)} %convolution_add_fusion.7), channel_id=1, source_target_pairs={{0,4},{4,8},{8,12},{12,16},{16,20},{20,24},{24,28},{1,5},{5,9},{9,... | collective-permute-start | bytes 393224 | tf_op jit(solution)/shard_map/while/body/eval_jaxpr/ppermute | solution.py:67
  92.8 2.8 %collective-permute-done = f32[64,512]{1,0:T(8,128)S(1)} collective-permute-done((f32[64,512]{1,0:T(8,128)}, f32[64,512]{1,0:T(8,128)S(1)}, u32[]{:S(2)}, u32[]{:S(2)}) %collective-permute-start) | collective-permute-done | bytes 131104 | tf_op jit(solution)/shard_map/while/body/eval_jaxpr/ppermute | solution.py:67
  95.7 1.7 convolution_add_fusion.6
  97.3 2.3 %convolution_add_fusion.7 = f32[64,512]{1,0:T(8,128)} fusion(f32[64,512]{1,0:T(8,128)S(1)} %convolution_add_fusion.6, f32[2,512,512]{2,1,0:T(8,128)S(1)} %get-tuple-element.167, f32[2,64,512]{2,1,0:T(8,128)} %get-tuple-element.168), kind=kOutput, calls=%fused_computation.clone.1 | convolution fusion | flops 201359360 | bytes 1441792 | tf_op jit(solution)/shard_map/while/body/eval_jaxpr/dot_general | solution.py:10
  99.6 5.1 %collective-permute-start = (f32[64,512]{1,0:T(8,128)}, f32[64,512]{1,0:T(8,128)S(1)}, u32[]{:S(2)}, u32[]{:S(2)}) collective-permute-start(f32[64,512]{1,0:T(8,128)} %convolution_add_fusion.7), channel_id=1, source_target_pairs={{0,4},{4,8},{8,12},{12,16},{16,20},{20,24},{24,28},{1,5},{5,9},{9,... | collective-permute-start | bytes 393224 | tf_op jit(solution)/shard_map/while/body/eval_jaxpr/ppermute | solution.py:67
  104.8 2.8 %collective-permute-done = f32[64,512]{1,0:T(8,128)S(1)} collective-permute-done((f32[64,512]{1,0:T(8,128)}, f32[64,512]{1,0:T(8,128)S(1)}, u32[]{:S(2)}, u32[]{:S(2)}) %collective-permute-start) | collective-permute-done | bytes 131104 | tf_op jit(solution)/shard_map/while/body/eval_jaxpr/ppermute | solution.py:67
  107.6 1.7 convolution_add_fusion.6
  109.2 2.3 %convolution_add_fusion.7 = f32[64,512]{1,0:T(8,128)} fusion(f32[64,512]{1,0:T(8,128)S(1)} %convolution_add_fusion.6, f32[2,512,512]{2,1,0:T(8,128)S(1)} %get-tuple-element.167, f32[2,64,512]{2,1,0:T(8,128)} %get-tuple-element.168), kind=kOutput, calls=%fused_computation.clone.1 | convolution fusion | flops 201359360 | bytes 1441792 | tf_op jit(solution)/shard_map/while/body/eval_jaxpr/dot_general | solution.py:10
  111.5 5.1 %collective-permute-start = (f32[64,512]{1,0:T(8,128)}, f32[64,512]{1,0:T(8,128)S(1)}, u32[]{:S(2)}, u32[]{:S(2)}) collective-permute-start(f32[64,512]{1,0:T(8,128)} %convolution_add_fusion.7), channel_id=1, source_target_pairs={{0,4},{4,8},{8,12},{12,16},{16,20},{20,24},{24,28},{1,5},{5,9},{9,... | collective-permute-start | bytes 393224 | tf_op jit(solution)/shard_map/while/body/eval_jaxpr/ppermute | solution.py:67
  116.7 2.8 %collective-permute-done = f32[64,512]{1,0:T(8,128)S(1)} collective-permute-done((f32[64,512]{1,0:T(8,128)}, f32[64,512]{1,0:T(8,128)S(1)}, u32[]{:S(2)}, u32[]{:S(2)}) %collective-permute-start) | collective-permute-done | bytes 131104 | tf_op jit(solution)/shard_map/while/body/eval_jaxpr/ppermute | solution.py:67
  120.1 2.4 %convolution_add_fusion.3 = f32[64,512]{1,0:T(8,128)S(1)} fusion(f32[64,512]{1,0:T(8,128)} %copy-done.1, f32[64,8,4,128]{3,2,1,0:T(4,128)} %bitcast.120, f32[8,8,4,128]{3,2,1,0:T(4,128)} %bitcast.124), kind=kOutput, calls=%fused_computation.18 | convolution fusion | flops 201359360 | bytes 1441792 | tf_op jit(solution)/shard_map/dot_general | solution.py:10
  122.5 2.7 %convolution_add_fusion.2 = f32[64,512]{1,0:T(8,128)} fusion(f32[64,512]{1,0:T(8,128)S(1)} %convolution_add_fusion.3, f32[64,8,4,128]{3,2,1,0:T(4,128)S(1)} %bitcast.117, f32[8,8,4,128]{3,2,1,0:T(4,128)} %bitcast.123), kind=kOutput, calls=%fused_computation.17 | convolution fusion | flops 201359360 | bytes 1441792 | tf_op jit(solution)/shard_map/dot_general | solution.py:10
  125.8 85.9 %while.21 = (s32[]{:T(128)}, f32[64,512]{1,0:T(8,128)}, f32[64,512]{1,0:T(8,128)}, f32[2,512,512]{2,1,0:T(8,128)S(1)}, f32[64,512]{1,0:T(8,128)S(1)}, /*index=5*/s32[]{:T(128)}) while((s32[]{:T(128)}, f32[64,512]{1,0:T(8,128)}, f32[64,512]{1,0:T(8,128)}, f32[2,512,512]{2,1,0:T(8,128)S(1)}, f32[64,512]{1,0:T(8,128)S(1)}, ...), condition=%wide.region_3.0_spmd, body=%wide.region_2.0_spmd.sunk | while | flops 402784256 | bytes 3407981 | solution.py:84
  125.8 2.1 fusion.63
  127.9 1.8 fusion.64
  129.7 1.3 collective-permute-start.1
  131.0 7.1 %collective-permute-done.1 = f32[64,512]{1,0:T(8,128)} collective-permute-done((f32[64,512]{1,0:T(8,128)}, f32[64,512]{1,0:T(8,128)}, u32[]{:S(2)}, u32[]{:S(2)}) %collective-permute-start.1) | collective-permute-done | bytes 131104 | tf_op jit(solution)/shard_map/while/body/eval_jaxpr/ppermute | solution.py:81
  138.1 2.1 fusion.63
  140.2 1.8 fusion.64
  142.0 1.3 collective-permute-start.1
  143.2 7.1 %collective-permute-done.1 = f32[64,512]{1,0:T(8,128)} collective-permute-done((f32[64,512]{1,0:T(8,128)}, f32[64,512]{1,0:T(8,128)}, u32[]{:S(2)}, u32[]{:S(2)}) %collective-permute-start.1) | collective-permute-done | bytes 131104 | tf_op jit(solution)/shard_map/while/body/eval_jaxpr/ppermute | solution.py:81
  150.3 2.1 fusion.63
  152.4 1.8 fusion.64
  154.2 1.3 collective-permute-start.1
  155.5 7.6 %collective-permute-done.1 = f32[64,512]{1,0:T(8,128)} collective-permute-done((f32[64,512]{1,0:T(8,128)}, f32[64,512]{1,0:T(8,128)}, u32[]{:S(2)}, u32[]{:S(2)}) %collective-permute-start.1) | collective-permute-done | bytes 131104 | tf_op jit(solution)/shard_map/while/body/eval_jaxpr/ppermute | solution.py:81
  163.1 2.1 fusion.63
  165.2 1.8 fusion.64
  167.0 1.3 collective-permute-start.1
  168.3 7.9 %collective-permute-done.1 = f32[64,512]{1,0:T(8,128)} collective-permute-done((f32[64,512]{1,0:T(8,128)}, f32[64,512]{1,0:T(8,128)}, u32[]{:S(2)}, u32[]{:S(2)}) %collective-permute-start.1) | collective-permute-done | bytes 131104 | tf_op jit(solution)/shard_map/while/body/eval_jaxpr/ppermute | solution.py:81
  176.2 2.1 fusion.63
  178.3 1.8 fusion.64
  181.3 6.5 %collective-permute-done.1 = f32[64,512]{1,0:T(8,128)} collective-permute-done((f32[64,512]{1,0:T(8,128)}, f32[64,512]{1,0:T(8,128)}, u32[]{:S(2)}, u32[]{:S(2)}) %collective-permute-start.1) | collective-permute-done | bytes 131104 | tf_op jit(solution)/shard_map/while/body/eval_jaxpr/ppermute | solution.py:81
  187.8 2.1 fusion.63
  189.9 1.8 fusion.64
  193.0 6.8 %collective-permute-done.1 = f32[64,512]{1,0:T(8,128)} collective-permute-done((f32[64,512]{1,0:T(8,128)}, f32[64,512]{1,0:T(8,128)}, u32[]{:S(2)}, u32[]{:S(2)}) %collective-permute-start.1) | collective-permute-done | bytes 131104 | tf_op jit(solution)/shard_map/while/body/eval_jaxpr/ppermute | solution.py:81
  199.8 2.1 fusion.63
  201.9 1.8 fusion.64
  204.9 6.8 %collective-permute-done.1 = f32[64,512]{1,0:T(8,128)} collective-permute-done((f32[64,512]{1,0:T(8,128)}, f32[64,512]{1,0:T(8,128)}, u32[]{:S(2)}, u32[]{:S(2)}) %collective-permute-start.1) | collective-permute-done | bytes 131104 | tf_op jit(solution)/shard_map/while/body/eval_jaxpr/ppermute | solution.py:81
  (25 shorter events, 16.9 us)
Async XLA Ops:
  7.2 1.0 copy-start
  7.2 22.9 %all-gather.3.cloned.1.call-start = ((), (), s32[]{:S(2)}) async-start(), calls=%async_computation | async-start | bytes 1310720 | tf_op jit(solution)/shard_map/all_gather | solution.py:46
  42.9 6.8 %collective-permute-start = (f32[64,512]{1,0:T(8,128)}, f32[64,512]{1,0:T(8,128)S(1)}, u32[]{:S(2)}, u32[]{:S(2)}) collective-permute-start(f32[64,512]{1,0:T(8,128)} %convolution_add_fusion.7), channel_id=1, source_target_pairs={{0,4},{4,8},{8,12},{12,16},{16,20},{20,24},{24,28},{1,5},{5,9},{9,... | collective-permute-start | bytes 393224 | tf_op jit(solution)/shard_map/while/body/eval_jaxpr/ppermute | solution.py:67
  53.7 7.1 %collective-permute-start = (f32[64,512]{1,0:T(8,128)}, f32[64,512]{1,0:T(8,128)S(1)}, u32[]{:S(2)}, u32[]{:S(2)}) collective-permute-start(f32[64,512]{1,0:T(8,128)} %convolution_add_fusion.7), channel_id=1, source_target_pairs={{0,4},{4,8},{8,12},{12,16},{16,20},{20,24},{24,28},{1,5},{5,9},{9,... | collective-permute-start | bytes 393224 | tf_op jit(solution)/shard_map/while/body/eval_jaxpr/ppermute | solution.py:67
  64.7 7.1 %collective-permute-start = (f32[64,512]{1,0:T(8,128)}, f32[64,512]{1,0:T(8,128)S(1)}, u32[]{:S(2)}, u32[]{:S(2)}) collective-permute-start(f32[64,512]{1,0:T(8,128)} %convolution_add_fusion.7), channel_id=1, source_target_pairs={{0,4},{4,8},{8,12},{12,16},{16,20},{20,24},{24,28},{1,5},{5,9},{9,... | collective-permute-start | bytes 393224 | tf_op jit(solution)/shard_map/while/body/eval_jaxpr/ppermute | solution.py:67
  75.8 8.0 %collective-permute-start = (f32[64,512]{1,0:T(8,128)}, f32[64,512]{1,0:T(8,128)S(1)}, u32[]{:S(2)}, u32[]{:S(2)}) collective-permute-start(f32[64,512]{1,0:T(8,128)} %convolution_add_fusion.7), channel_id=1, source_target_pairs={{0,4},{4,8},{8,12},{12,16},{16,20},{20,24},{24,28},{1,5},{5,9},{9,... | collective-permute-start | bytes 393224 | tf_op jit(solution)/shard_map/while/body/eval_jaxpr/ppermute | solution.py:67
  87.7 8.0 %collective-permute-start = (f32[64,512]{1,0:T(8,128)}, f32[64,512]{1,0:T(8,128)S(1)}, u32[]{:S(2)}, u32[]{:S(2)}) collective-permute-start(f32[64,512]{1,0:T(8,128)} %convolution_add_fusion.7), channel_id=1, source_target_pairs={{0,4},{4,8},{8,12},{12,16},{16,20},{20,24},{24,28},{1,5},{5,9},{9,... | collective-permute-start | bytes 393224 | tf_op jit(solution)/shard_map/while/body/eval_jaxpr/ppermute | solution.py:67
  99.6 8.0 %collective-permute-start = (f32[64,512]{1,0:T(8,128)}, f32[64,512]{1,0:T(8,128)S(1)}, u32[]{:S(2)}, u32[]{:S(2)}) collective-permute-start(f32[64,512]{1,0:T(8,128)} %convolution_add_fusion.7), channel_id=1, source_target_pairs={{0,4},{4,8},{8,12},{12,16},{16,20},{20,24},{24,28},{1,5},{5,9},{9,... | collective-permute-start | bytes 393224 | tf_op jit(solution)/shard_map/while/body/eval_jaxpr/ppermute | solution.py:67
  111.5 8.0 %collective-permute-start = (f32[64,512]{1,0:T(8,128)}, f32[64,512]{1,0:T(8,128)S(1)}, u32[]{:S(2)}, u32[]{:S(2)}) collective-permute-start(f32[64,512]{1,0:T(8,128)} %convolution_add_fusion.7), channel_id=1, source_target_pairs={{0,4},{4,8},{8,12},{12,16},{16,20},{20,24},{24,28},{1,5},{5,9},{9,... | collective-permute-start | bytes 393224 | tf_op jit(solution)/shard_map/while/body/eval_jaxpr/ppermute | solution.py:67
  119.5 0.6 copy-start.1
  129.7 8.4 %collective-permute-start.1 = (f32[64,512]{1,0:T(8,128)}, f32[64,512]{1,0:T(8,128)}, u32[]{:S(2)}, u32[]{:S(2)}) collective-permute-start(f32[64,512]{1,0:T(8,128)} %fusion.64), channel_id=1, source_target_pairs={{4,0},{8,4},{12,8},{16,12},{20,16},{24,20},{28,24},{5,1},{9,5},{13... | collective-permute-start | bytes 393224 | tf_op jit(solution)/shard_map/while/body/eval_jaxpr/ppermute | solution.py:81
  142.0 8.4 %collective-permute-start.1 = (f32[64,512]{1,0:T(8,128)}, f32[64,512]{1,0:T(8,128)}, u32[]{:S(2)}, u32[]{:S(2)}) collective-permute-start(f32[64,512]{1,0:T(8,128)} %fusion.64), channel_id=1, source_target_pairs={{4,0},{8,4},{12,8},{16,12},{20,16},{24,20},{28,24},{5,1},{9,5},{13... | collective-permute-start | bytes 393224 | tf_op jit(solution)/shard_map/while/body/eval_jaxpr/ppermute | solution.py:81
  154.2 8.9 %collective-permute-start.1 = (f32[64,512]{1,0:T(8,128)}, f32[64,512]{1,0:T(8,128)}, u32[]{:S(2)}, u32[]{:S(2)}) collective-permute-start(f32[64,512]{1,0:T(8,128)} %fusion.64), channel_id=1, source_target_pairs={{4,0},{8,4},{12,8},{16,12},{20,16},{24,20},{28,24},{5,1},{9,5},{13... | collective-permute-start | bytes 393224 | tf_op jit(solution)/shard_map/while/body/eval_jaxpr/ppermute | solution.py:81
  167.0 9.2 %collective-permute-start.1 = (f32[64,512]{1,0:T(8,128)}, f32[64,512]{1,0:T(8,128)}, u32[]{:S(2)}, u32[]{:S(2)}) collective-permute-start(f32[64,512]{1,0:T(8,128)} %fusion.64), channel_id=1, source_target_pairs={{4,0},{8,4},{12,8},{16,12},{20,16},{24,20},{28,24},{5,1},{9,5},{13... | collective-permute-start | bytes 393224 | tf_op jit(solution)/shard_map/while/body/eval_jaxpr/ppermute | solution.py:81
  180.1 7.8 %collective-permute-start.1 = (f32[64,512]{1,0:T(8,128)}, f32[64,512]{1,0:T(8,128)}, u32[]{:S(2)}, u32[]{:S(2)}) collective-permute-start(f32[64,512]{1,0:T(8,128)} %fusion.64), channel_id=1, source_target_pairs={{4,0},{8,4},{12,8},{16,12},{20,16},{24,20},{28,24},{5,1},{9,5},{13... | collective-permute-start | bytes 393224 | tf_op jit(solution)/shard_map/while/body/eval_jaxpr/ppermute | solution.py:81
  191.7 8.1 %collective-permute-start.1 = (f32[64,512]{1,0:T(8,128)}, f32[64,512]{1,0:T(8,128)}, u32[]{:S(2)}, u32[]{:S(2)}) collective-permute-start(f32[64,512]{1,0:T(8,128)} %fusion.64), channel_id=1, source_target_pairs={{4,0},{8,4},{12,8},{16,12},{20,16},{24,20},{28,24},{5,1},{9,5},{13... | collective-permute-start | bytes 393224 | tf_op jit(solution)/shard_map/while/body/eval_jaxpr/ppermute | solution.py:81
  203.6 8.1 %collective-permute-start.1 = (f32[64,512]{1,0:T(8,128)}, f32[64,512]{1,0:T(8,128)}, u32[]{:S(2)}, u32[]{:S(2)}) collective-permute-start(f32[64,512]{1,0:T(8,128)} %fusion.64), channel_id=1, source_target_pairs={{4,0},{8,4},{12,8},{16,12},{20,16},{24,20},{28,24},{5,1},{9,5},{13... | collective-permute-start | bytes 393224 | tf_op jit(solution)/shard_map/while/body/eval_jaxpr/ppermute | solution.py:81
Sparse Core Ops, SparseCore 0:
  10.6 19.4 all-gather.2
where the time goes:
time: 226 us; the launch traced here: 224 us
  waiting for transfers between devices  78.1 us (35%)
  matrix products  69.3 us (31%)
  starting transfers between devices  41.5 us (18%)
  between operations  14.1 us (6%)
  local copies, waits for them, and re-layouts  11.8 us (5%)
  blocking collectives  7.25 us (3%)
    ppermute x7, waiting for transfers between devices, backward_hop(): return lax.ppermute(backward_levels(running)[1], 'chain', behind)  49.8 us
    dot_general x18, matrix products, matmul(): jnp.dot(left_side, right_factor, precision=PRECISE, preferred_element_typ...  34.8 us
    ppermute x7, starting transfers between devices, forward_hop(): return lax.ppermute(forward_levels(state)[-1], 'chain', ahead)  32.5 us
    dot_general x15, matrix products, matmul_trans(): lax.dot_general(left_side, right_factor, (((1,), (1,)), ((), ())), precis...  27.8 us
    ppermute x7, waiting for transfers between devices, forward_hop(): return lax.ppermute(forward_levels(state)[-1], 'chain', ahead)  20.3 us
    ppermute x7, starting transfers between devices, backward_hop(): return lax.ppermute(backward_levels(running)[1], 'chain', behind)  8.96 us
    all_gather x1, waiting for transfers between devices, shards(): lax.all_gather(scaled, 'grp', axis=1, tiled=True)  8 us
    all_gather x1, blocking collectives, shards(): lax.all_gather(lifted, 'grp', axis=1, tiled=True)  7.25 us
  transfers between devices with their start and end apart: 15, of which 15 were waited for; matrix products, arithmetic and copies ran while one was open for 2% of the time, Pallas kernels for 0%

commit v1 on v0

--- a/solution.py
+++ b/solution.py
@@ -4,6 +4,37 @@
 from jax.sharding import PartitionSpec as P
 
 PRECISE = lax.Precision.HIGHEST
+
+
+def point_column(content, dimension_no):
+    raw_out = list(content.shape[1:])
+    raw_out[dimension_no] *= content.shape[0]
+    local_next = jnp.moveaxis(content, 0, dimension_no).reshape(raw_out)
+    return local_next
+
+
+def make_the_routes_all(inner_x, mesh_dim, in_dim=1):
+    axis_total = lax.axis_size(mesh_dim)
+    pool = list(map(lambda num: (num, (num + 1) % axis_total), range(axis_total)))
+    windows = [(dd, i0) for i0, dd in pool]
+    u_next, passed = ([], [])
+    nth = 0
+    while nth < axis_total - 1:
+        if nth % 2 == 0:
+            wide_out = lax.ppermute(u_next[-1] if u_next else inner_x, mesh_dim, pool)
+            u_next.append(wide_out)
+        else:
+            all_values = lax.ppermute(
+                passed[-1] if passed else inner_x, perm=windows, axis_name=mesh_dim
+            )
+            passed.append(all_values)
+        nth += 1
+    view_out = jnp.stack([*u_next[::-1], inner_x, *passed], 0)
+    far_arr = lax.axis_index(mesh_dim)
+    b_next = far_arr - len(u_next)
+    view_out = view_out[(jnp.arange(axis_total) - b_next) % axis_total]
+    out_arr = point_column(view_out, in_dim)
+    return out_arr
 
 
 def matmul(left_side, right_factor):
@@ -43,7 +74,7 @@
         preferred_element_type=jnp.float32,
     )
     blocks, offsets = (
-        lax.all_gather(scaled, "grp", axis=1, tiled=True),
+        make_the_routes_all(scaled, "grp"),
         lax.all_gather(lifted, "grp", axis=1, tiled=True),
     )
     onehot = (pattern[..., None] == jnp.arange(groups, dtype=jnp.int32)).astype(jnp.float32)

time: 226 us -> 209 us (0.925)
  between operations: 14.1 us -> 0.75 us
  waiting for transfers between devices: 78.1 us -> 72.6 us
  starting transfers between devices: 41.5 us -> 44.7 us
    all_gather x1 -> x0, waiting for transfers between devices: 8 us -> none  [shards(): lax.all_gather(scaled, 'grp', axis=1, tiled=True)]
    ppermute x0 -> x3, waiting for transfers between devices: none -> 2.91 us  [the longest x2 2.9 us: make_the_routes_all(): wide_out = lax.ppermute(u_next[-1] if u_next else inner_x, mesh_dim, pool)]
    ppermute x0 -> x3, starting transfers between devices: none -> 2.9 us  [the longest x1 2.01 us: make_the_routes_all(): lax.ppermute(passed[-1] if passed else inner_x, perm=windows, axis_name=m...]
  transfers between devices with their start and end apart: 15 -> 17, of which waited for: 15 -> 15; matrix products, arithmetic and copies ran while one was open for 2% -> 2% of each run, Pallas kernels for 0% -> 0%
where the time goes in v1:
time: 209 us; the launch traced here: 208 us
  waiting for transfers between devices  72.6 us (35%)
  matrix products  67.7 us (32%)
  starting transfers between devices  44.7 us (21%)
  local copies, waits for them, and re-layouts  12.2 us (6%)
  blocking collectives  7.74 us (4%)
  other arithmetic  2.37 us (1%)
    ppermute x7, waiting for transfers between devices, backward_hop(): return lax.ppermute(backward_levels(running)[1], 'chain', behind)  50 us
    dot_general x18, matrix products, matmul(): jnp.dot(left_side, right_factor, precision=PRECISE, preferred_element_typ...  34.8 us
    ppermute x7, starting transfers between devices, forward_hop(): return lax.ppermute(forward_levels(state)[-1], 'chain', ahead)  32.8 us
    dot_general x15, matrix products, matmul_trans(): lax.dot_general(left_side, right_factor, (((1,), (1,)), ((), ())), precis...  27.8 us
    ppermute x7, waiting for transfers between devices, forward_hop(): return lax.ppermute(forward_levels(state)[-1], 'chain', ahead)  19.7 us
    ppermute x7, starting transfers between devices, backward_hop(): return lax.ppermute(backward_levels(running)[1], 'chain', behind)  8.96 us
    all_gather x1, blocking collectives, shards(): lax.all_gather(lifted, 'grp', axis=1, tiled=True)  7.74 us
  transfers between devices with their start and end apart: 17, of which 15 were waited for; matrix products, arithmetic and copies ran while one was open for 2% of the time, Pallas kernels for 0%

profile of v1, /device:TPU:0, one launch (start us, length us, event | category | flops | bytes accessed | tf_op | source)
XLA Modules:
  0.0 208.3 jit_solution(10255835644407514875)
XLA Ops:
  1.6 1.5 fusion.19
  3.6 2.0 collective-permute-start.4
  5.6 1.3 fusion.22
  6.9 7.7 %all-gather = f32[2,256,128]{2,1,0:T(8,128)S(1)} all-gather(f32[2,64,128]{2,1,0:T(8,128)S(1)} %fusion.22), channel_id=2, replica_groups=mesh['chain'=8,'grp'=4] {'grp'}, dimensions={1}, use_global_device_ids=true | all-gather | bytes 327680 | tf_op jit(solution)/shard_map/all_gather | solution.py:78
  18.1 2.9 %collective-permute-done.3 = f32[2,1,2,128,128]{3,4,2,0,1:T(8,128)S(1)} collective-permute-done((f32[2,1,2,128,128]{3,4,2,0,1:T(8,128)S(1)}, f32[2,1,2,128,128]{3,4,2,0,1:T(8,128)S(1)}, u32[]{:S(2)}, u32[]{:S(2)}) %collective-permute-start.3) | collective-permute-done | bytes 262176 | tf_op jit(solution)/shard_map/ppermute | solution.py:24
  22.3 2.4 %negate_bitcast_fusion = f32[2,4,128,4,128]{2,1,4,3,0:T(4,128)S(1)} fusion(f32[2,4,2,128,128]{4,2,3,1,0:T(2,128)S(1)} %copy.8, s32[2,4,2]{2,1,0:T(4,128)S(1)} %copy.7), kind=kOutput, calls=%fused_computation.16 | convolution fusion | flops 13107264 | bytes 3145792 | tf_op jit(solution)/shard_map/lgkh,lgktj->lhjgt/dot_general | solution.py:81
  24.7 1.9 reshape.86
  27.7 1.9 copy.10
  29.7 80.3 %while.20 = (s32[]{:T(128)}, f32[64,512]{1,0:T(8,128)S(1)}, f32[2,512,512]{2,1,0:T(8,128)S(1)}, f32[2,64,512]{2,1,0:T(8,128)}, s32[]{:T(128)}) while((s32[]{:T(128)}, f32[64,512]{1,0:T(8,128)S(1)}, f32[2,512,512]{2,1,0:T(8,128)S(1)}, f32[2,64,512]{2,1,0:T(8,128)}, s32[]{:T(128)}) %tuple.48), condition=%wide.region_1.2_spmd, body=%wide.region_0.1_spmd.sunk | while | flops 402718720 | bytes 3407973 | solution.py:101
  29.7 1.7 convolution_add_fusion.6
  31.3 2.3 %convolution_add_fusion.7 = f32[64,512]{1,0:T(8,128)} fusion(f32[64,512]{1,0:T(8,128)S(1)} %convolution_add_fusion.6, f32[2,512,512]{2,1,0:T(8,128)S(1)} %get-tuple-element.156, f32[2,64,512]{2,1,0:T(8,128)} %get-tuple-element.157), kind=kOutput, calls=%fused_computation.1.clone.1 | convolution fusion | flops 201359360 | bytes 1441792 | tf_op jit(solution)/shard_map/while/body/eval_jaxpr/dot_general | solution.py:41
  33.6 3.7 %collective-permute-start = (f32[64,512]{1,0:T(8,128)}, f32[64,512]{1,0:T(8,128)S(1)}, u32[]{:S(2)}, u32[]{:S(2)}) collective-permute-start(f32[64,512]{1,0:T(8,128)} %convolution_add_fusion.7), channel_id=1, source_target_pairs={{0,4},{4,8},{8,12},{12,16},{16,20},{20,24},{24,28},{1,5},{5,9},{9,... | collective-permute-start | bytes 393224 | tf_op jit(solution)/shard_map/while/body/eval_jaxpr/ppermute | solution.py:98
  37.3 2.8 %collective-permute-done = f32[64,512]{1,0:T(8,128)S(1)} collective-permute-done((f32[64,512]{1,0:T(8,128)}, f32[64,512]{1,0:T(8,128)S(1)}, u32[]{:S(2)}, u32[]{:S(2)}) %collective-permute-start) | collective-permute-done | bytes 131104 | tf_op jit(solution)/shard_map/while/body/eval_jaxpr/ppermute | solution.py:98
  40.1 1.7 convolution_add_fusion.6
  41.8 2.3 %convolution_add_fusion.7 = f32[64,512]{1,0:T(8,128)} fusion(f32[64,512]{1,0:T(8,128)S(1)} %convolution_add_fusion.6, f32[2,512,512]{2,1,0:T(8,128)S(1)} %get-tuple-element.156, f32[2,64,512]{2,1,0:T(8,128)} %get-tuple-element.157), kind=kOutput, calls=%fused_computation.1.clone.1 | convolution fusion | flops 201359360 | bytes 1441792 | tf_op jit(solution)/shard_map/while/body/eval_jaxpr/dot_general | solution.py:41
  44.1 4.2 %collective-permute-start = (f32[64,512]{1,0:T(8,128)}, f32[64,512]{1,0:T(8,128)S(1)}, u32[]{:S(2)}, u32[]{:S(2)}) collective-permute-start(f32[64,512]{1,0:T(8,128)} %convolution_add_fusion.7), channel_id=1, source_target_pairs={{0,4},{4,8},{8,12},{12,16},{16,20},{20,24},{24,28},{1,5},{5,9},{9,... | collective-permute-start | bytes 393224 | tf_op jit(solution)/shard_map/while/body/eval_jaxpr/ppermute | solution.py:98
  48.3 2.8 %collective-permute-done = f32[64,512]{1,0:T(8,128)S(1)} collective-permute-done((f32[64,512]{1,0:T(8,128)}, f32[64,512]{1,0:T(8,128)S(1)}, u32[]{:S(2)}, u32[]{:S(2)}) %collective-permute-start) | collective-permute-done | bytes 131104 | tf_op jit(solution)/shard_map/while/body/eval_jaxpr/ppermute | solution.py:98
  51.1 1.7 convolution_add_fusion.6
  52.8 2.3 %convolution_add_fusion.7 = f32[64,512]{1,0:T(8,128)} fusion(f32[64,512]{1,0:T(8,128)S(1)} %convolution_add_fusion.6, f32[2,512,512]{2,1,0:T(8,128)S(1)} %get-tuple-element.156, f32[2,64,512]{2,1,0:T(8,128)} %get-tuple-element.157), kind=kOutput, calls=%fused_computation.1.clone.1 | convolution fusion | flops 201359360 | bytes 1441792 | tf_op jit(solution)/shard_map/while/body/eval_jaxpr/dot_general | solution.py:41
  55.1 4.3 %collective-permute-start = (f32[64,512]{1,0:T(8,128)}, f32[64,512]{1,0:T(8,128)S(1)}, u32[]{:S(2)}, u32[]{:S(2)}) collective-permute-start(f32[64,512]{1,0:T(8,128)} %convolution_add_fusion.7), channel_id=1, source_target_pairs={{0,4},{4,8},{8,12},{12,16},{16,20},{20,24},{24,28},{1,5},{5,9},{9,... | collective-permute-start | bytes 393224 | tf_op jit(solution)/shard_map/while/body/eval_jaxpr/ppermute | solution.py:98
  59.4 2.8 %collective-permute-done = f32[64,512]{1,0:T(8,128)S(1)} collective-permute-done((f32[64,512]{1,0:T(8,128)}, f32[64,512]{1,0:T(8,128)S(1)}, u32[]{:S(2)}, u32[]{:S(2)}) %collective-permute-start) | collective-permute-done | bytes 131104 | tf_op jit(solution)/shard_map/while/body/eval_jaxpr/ppermute | solution.py:98
  62.3 1.7 convolution_add_fusion.6
  63.9 2.3 %convolution_add_fusion.7 = f32[64,512]{1,0:T(8,128)} fusion(f32[64,512]{1,0:T(8,128)S(1)} %convolution_add_fusion.6, f32[2,512,512]{2,1,0:T(8,128)S(1)} %get-tuple-element.156, f32[2,64,512]{2,1,0:T(8,128)} %get-tuple-element.157), kind=kOutput, calls=%fused_computation.1.clone.1 | convolution fusion | flops 201359360 | bytes 1441792 | tf_op jit(solution)/shard_map/while/body/eval_jaxpr/dot_general | solution.py:41
  66.2 5.1 %collective-permute-start = (f32[64,512]{1,0:T(8,128)}, f32[64,512]{1,0:T(8,128)S(1)}, u32[]{:S(2)}, u32[]{:S(2)}) collective-permute-start(f32[64,512]{1,0:T(8,128)} %convolution_add_fusion.7), channel_id=1, source_target_pairs={{0,4},{4,8},{8,12},{12,16},{16,20},{20,24},{24,28},{1,5},{5,9},{9,... | collective-permute-start | bytes 393224 | tf_op jit(solution)/shard_map/while/body/eval_jaxpr/ppermute | solution.py:98
  71.4 2.8 %collective-permute-done = f32[64,512]{1,0:T(8,128)S(1)} collective-permute-done((f32[64,512]{1,0:T(8,128)}, f32[64,512]{1,0:T(8,128)S(1)}, u32[]{:S(2)}, u32[]{:S(2)}) %collective-permute-start) | collective-permute-done | bytes 131104 | tf_op jit(solution)/shard_map/while/body/eval_jaxpr/ppermute | solution.py:98
  74.2 1.7 convolution_add_fusion.6
  75.8 2.3 %convolution_add_fusion.7 = f32[64,512]{1,0:T(8,128)} fusion(f32[64,512]{1,0:T(8,128)S(1)} %convolution_add_fusion.6, f32[2,512,512]{2,1,0:T(8,128)S(1)} %get-tuple-element.156, f32[2,64,512]{2,1,0:T(8,128)} %get-tuple-element.157), kind=kOutput, calls=%fused_computation.1.clone.1 | convolution fusion | flops 201359360 | bytes 1441792 | tf_op jit(solution)/shard_map/while/body/eval_jaxpr/dot_general | solution.py:41
  78.1 5.1 %collective-permute-start = (f32[64,512]{1,0:T(8,128)}, f32[64,512]{1,0:T(8,128)S(1)}, u32[]{:S(2)}, u32[]{:S(2)}) collective-permute-start(f32[64,512]{1,0:T(8,128)} %convolution_add_fusion.7), channel_id=1, source_target_pairs={{0,4},{4,8},{8,12},{12,16},{16,20},{20,24},{24,28},{1,5},{5,9},{9,... | collective-permute-start | bytes 393224 | tf_op jit(solution)/shard_map/while/body/eval_jaxpr/ppermute | solution.py:98
  83.3 2.8 %collective-permute-done = f32[64,512]{1,0:T(8,128)S(1)} collective-permute-done((f32[64,512]{1,0:T(8,128)}, f32[64,512]{1,0:T(8,128)S(1)}, u32[]{:S(2)}, u32[]{:S(2)}) %collective-permute-start) | collective-permute-done | bytes 131104 | tf_op jit(solution)/shard_map/while/body/eval_jaxpr/ppermute | solution.py:98
  86.1 1.7 convolution_add_fusion.6
  87.7 2.3 %convolution_add_fusion.7 = f32[64,512]{1,0:T(8,128)} fusion(f32[64,512]{1,0:T(8,128)S(1)} %convolution_add_fusion.6, f32[2,512,512]{2,1,0:T(8,128)S(1)} %get-tuple-element.156, f32[2,64,512]{2,1,0:T(8,128)} %get-tuple-element.157), kind=kOutput, calls=%fused_computation.1.clone.1 | convolution fusion | flops 201359360 | bytes 1441792 | tf_op jit(solution)/shard_map/while/body/eval_jaxpr/dot_general | solution.py:41
  90.1 5.1 %collective-permute-start = (f32[64,512]{1,0:T(8,128)}, f32[64,512]{1,0:T(8,128)S(1)}, u32[]{:S(2)}, u32[]{:S(2)}) collective-permute-start(f32[64,512]{1,0:T(8,128)} %convolution_add_fusion.7), channel_id=1, source_target_pairs={{0,4},{4,8},{8,12},{12,16},{16,20},{20,24},{24,28},{1,5},{5,9},{9,... | collective-permute-start | bytes 393224 | tf_op jit(solution)/shard_map/while/body/eval_jaxpr/ppermute | solution.py:98
  95.2 2.8 %collective-permute-done = f32[64,512]{1,0:T(8,128)S(1)} collective-permute-done((f32[64,512]{1,0:T(8,128)}, f32[64,512]{1,0:T(8,128)S(1)}, u32[]{:S(2)}, u32[]{:S(2)}) %collective-permute-start) | collective-permute-done | bytes 131104 | tf_op jit(solution)/shard_map/while/body/eval_jaxpr/ppermute | solution.py:98
  98.0 1.7 convolution_add_fusion.6
  99.7 2.3 %convolution_add_fusion.7 = f32[64,512]{1,0:T(8,128)} fusion(f32[64,512]{1,0:T(8,128)S(1)} %convolution_add_fusion.6, f32[2,512,512]{2,1,0:T(8,128)S(1)} %get-tuple-element.156, f32[2,64,512]{2,1,0:T(8,128)} %get-tuple-element.157), kind=kOutput, calls=%fused_computation.1.clone.1 | convolution fusion | flops 201359360 | bytes 1441792 | tf_op jit(solution)/shard_map/while/body/eval_jaxpr/dot_general | solution.py:41
  102.0 5.1 %collective-permute-start = (f32[64,512]{1,0:T(8,128)}, f32[64,512]{1,0:T(8,128)S(1)}, u32[]{:S(2)}, u32[]{:S(2)}) collective-permute-start(f32[64,512]{1,0:T(8,128)} %convolution_add_fusion.7), channel_id=1, source_target_pairs={{0,4},{4,8},{8,12},{12,16},{16,20},{20,24},{24,28},{1,5},{5,9},{9,... | collective-permute-start | bytes 393224 | tf_op jit(solution)/shard_map/while/body/eval_jaxpr/ppermute | solution.py:98
  107.1 2.8 %collective-permute-done = f32[64,512]{1,0:T(8,128)S(1)} collective-permute-done((f32[64,512]{1,0:T(8,128)}, f32[64,512]{1,0:T(8,128)S(1)}, u32[]{:S(2)}, u32[]{:S(2)}) %collective-permute-start) | collective-permute-done | bytes 131104 | tf_op jit(solution)/shard_map/while/body/eval_jaxpr/ppermute | solution.py:98
  110.6 2.4 %convolution_add_fusion.3 = f32[64,512]{1,0:T(8,128)S(1)} fusion(f32[64,512]{1,0:T(8,128)} %copy-done.1, f32[64,8,4,128]{3,2,1,0:T(4,128)} %bitcast.135, f32[8,8,4,128]{3,2,1,0:T(4,128)} %bitcast.142), kind=kOutput, calls=%fused_computation.18 | convolution fusion | flops 201359360 | bytes 1441792 | tf_op jit(solution)/shard_map/dot_general | solution.py:41
  112.9 2.7 %convolution_add_fusion.2 = f32[64,512]{1,0:T(8,128)} fusion(f32[64,512]{1,0:T(8,128)S(1)} %convolution_add_fusion.3, f32[64,8,4,128]{3,2,1,0:T(4,128)S(1)} %bitcast.131, f32[8,8,4,128]{3,2,1,0:T(4,128)} %bitcast.141), kind=kOutput, calls=%fused_computation.17 | convolution fusion | flops 201359360 | bytes 1441792 | tf_op jit(solution)/shard_map/dot_general | solution.py:41
  116.3 86.2 %while.21 = (s32[]{:T(128)}, f32[64,512]{1,0:T(8,128)}, f32[64,512]{1,0:T(8,128)}, f32[2,512,512]{2,1,0:T(8,128)S(1)}, f32[64,512]{1,0:T(8,128)S(1)}, /*index=5*/s32[]{:T(128)}) while((s32[]{:T(128)}, f32[64,512]{1,0:T(8,128)}, f32[64,512]{1,0:T(8,128)}, f32[2,512,512]{2,1,0:T(8,128)S(1)}, f32[64,512]{1,0:T(8,128)S(1)}, ...), condition=%wide.region_3.4_spmd, body=%wide.region_2.3_spmd.sunk | while | flops 402784256 | bytes 3407981 | solution.py:115
  116.3 2.1 %fusion.66 = f32[64,512]{1,0:T(8,128)S(1)} fusion(f32[64,512]{1,0:T(8,128)S(1)} %get-tuple-element.175, f32[2,512,512]{2,1,0:T(8,128)S(1)} %get-tuple-element.174, f32[64,512]{1,0:T(8,128)} %get-tuple-element.173, f32[64,512]{1,0:T(8,128)} %get-tuple-element.166), kind=kOutput, calls=%fused_computation.8.clone.1 | convolution fusion | flops 201457664 | bytes 1572864 | tf_op jit(solution)/shard_map/while/body/eval_jaxpr/dot_general | solution.py:45
  118.4 1.8 fusion.67
  120.1 1.3 collective-permute-start.1
  121.4 7.1 %collective-permute-done.1 = f32[64,512]{1,0:T(8,128)} collective-permute-done((f32[64,512]{1,0:T(8,128)}, f32[64,512]{1,0:T(8,128)}, u32[]{:S(2)}, u32[]{:S(2)}) %collective-permute-start.1) | collective-permute-done | bytes 131104 | tf_op jit(solution)/shard_map/while/body/eval_jaxpr/ppermute | solution.py:112
  128.5 2.1 %fusion.66 = f32[64,512]{1,0:T(8,128)S(1)} fusion(f32[64,512]{1,0:T(8,128)S(1)} %get-tuple-element.175, f32[2,512,512]{2,1,0:T(8,128)S(1)} %get-tuple-element.174, f32[64,512]{1,0:T(8,128)} %get-tuple-element.173, f32[64,512]{1,0:T(8,128)} %get-tuple-element.166), kind=kOutput, calls=%fused_computation.8.clone.1 | convolution fusion | flops 201457664 | bytes 1572864 | tf_op jit(solution)/shard_map/while/body/eval_jaxpr/dot_general | solution.py:45
  130.6 1.8 fusion.67
  132.4 1.3 collective-permute-start.1
  133.7 8.4 %collective-permute-done.1 = f32[64,512]{1,0:T(8,128)} collective-permute-done((f32[64,512]{1,0:T(8,128)}, f32[64,512]{1,0:T(8,128)}, u32[]{:S(2)}, u32[]{:S(2)}) %collective-permute-start.1) | collective-permute-done | bytes 131104 | tf_op jit(solution)/shard_map/while/body/eval_jaxpr/ppermute | solution.py:112
  142.1 2.1 %fusion.66 = f32[64,512]{1,0:T(8,128)S(1)} fusion(f32[64,512]{1,0:T(8,128)S(1)} %get-tuple-element.175, f32[2,512,512]{2,1,0:T(8,128)S(1)} %get-tuple-element.174, f32[64,512]{1,0:T(8,128)} %get-tuple-element.173, f32[64,512]{1,0:T(8,128)} %get-tuple-element.166), kind=kOutput, calls=%fused_computation.8.clone.1 | convolution fusion | flops 201457664 | bytes 1572864 | tf_op jit(solution)/shard_map/while/body/eval_jaxpr/dot_general | solution.py:45
  144.2 1.8 fusion.67
  145.9 1.3 collective-permute-start.1
  147.2 7.7 %collective-permute-done.1 = f32[64,512]{1,0:T(8,128)} collective-permute-done((f32[64,512]{1,0:T(8,128)}, f32[64,512]{1,0:T(8,128)}, u32[]{:S(2)}, u32[]{:S(2)}) %collective-permute-start.1) | collective-permute-done | bytes 131104 | tf_op jit(solution)/shard_map/while/body/eval_jaxpr/ppermute | solution.py:112
  155.0 2.1 %fusion.66 = f32[64,512]{1,0:T(8,128)S(1)} fusion(f32[64,512]{1,0:T(8,128)S(1)} %get-tuple-element.175, f32[2,512,512]{2,1,0:T(8,128)S(1)} %get-tuple-element.174, f32[64,512]{1,0:T(8,128)} %get-tuple-element.173, f32[64,512]{1,0:T(8,128)} %get-tuple-element.166), kind=kOutput, calls=%fused_computation.8.clone.1 | convolution fusion | flops 201457664 | bytes 1572864 | tf_op jit(solution)/shard_map/while/body/eval_jaxpr/dot_general | solution.py:45
  157.1 1.8 fusion.67
  160.1 6.5 %collective-permute-done.1 = f32[64,512]{1,0:T(8,128)} collective-permute-done((f32[64,512]{1,0:T(8,128)}, f32[64,512]{1,0:T(8,128)}, u32[]{:S(2)}, u32[]{:S(2)}) %collective-permute-start.1) | collective-permute-done | bytes 131104 | tf_op jit(solution)/shard_map/while/body/eval_jaxpr/ppermute | solution.py:112
  166.6 2.1 %fusion.66 = f32[64,512]{1,0:T(8,128)S(1)} fusion(f32[64,512]{1,0:T(8,128)S(1)} %get-tuple-element.175, f32[2,512,512]{2,1,0:T(8,128)S(1)} %get-tuple-element.174, f32[64,512]{1,0:T(8,128)} %get-tuple-element.173, f32[64,512]{1,0:T(8,128)} %get-tuple-element.166), kind=kOutput, calls=%fused_computation.8.clone.1 | convolution fusion | flops 201457664 | bytes 1572864 | tf_op jit(solution)/shard_map/while/body/eval_jaxpr/dot_general | solution.py:45
  168.7 1.8 fusion.67
  171.8 6.8 %collective-permute-done.1 = f32[64,512]{1,0:T(8,128)} collective-permute-done((f32[64,512]{1,0:T(8,128)}, f32[64,512]{1,0:T(8,128)}, u32[]{:S(2)}, u32[]{:S(2)}) %collective-permute-start.1) | collective-permute-done | bytes 131104 | tf_op jit(solution)/shard_map/while/body/eval_jaxpr/ppermute | solution.py:112
  178.6 2.1 %fusion.66 = f32[64,512]{1,0:T(8,128)S(1)} fusion(f32[64,512]{1,0:T(8,128)S(1)} %get-tuple-element.175, f32[2,512,512]{2,1,0:T(8,128)S(1)} %get-tuple-element.174, f32[64,512]{1,0:T(8,128)} %get-tuple-element.173, f32[64,512]{1,0:T(8,128)} %get-tuple-element.166), kind=kOutput, calls=%fused_computation.8.clone.1 | convolution fusion | flops 201457664 | bytes 1572864 | tf_op jit(solution)/shard_map/while/body/eval_jaxpr/dot_general | solution.py:45
  180.6 1.8 fusion.67
  183.7 6.8 %collective-permute-done.1 = f32[64,512]{1,0:T(8,128)} collective-permute-done((f32[64,512]{1,0:T(8,128)}, f32[64,512]{1,0:T(8,128)}, u32[]{:S(2)}, u32[]{:S(2)}) %collective-permute-start.1) | collective-permute-done | bytes 131104 | tf_op jit(solution)/shard_map/while/body/eval_jaxpr/ppermute | solution.py:112
  190.5 2.1 %fusion.66 = f32[64,512]{1,0:T(8,128)S(1)} fusion(f32[64,512]{1,0:T(8,128)S(1)} %get-tuple-element.175, f32[2,512,512]{2,1,0:T(8,128)S(1)} %get-tuple-element.174, f32[64,512]{1,0:T(8,128)} %get-tuple-element.173, f32[64,512]{1,0:T(8,128)} %get-tuple-element.166), kind=kOutput, calls=%fused_computation.8.clone.1 | convolution fusion | flops 201457664 | bytes 1572864 | tf_op jit(solution)/shard_map/while/body/eval_jaxpr/dot_general | solution.py:45
  192.6 1.8 fusion.67
  195.7 6.8 %collective-permute-done.1 = f32[64,512]{1,0:T(8,128)} collective-permute-done((f32[64,512]{1,0:T(8,128)}, f32[64,512]{1,0:T(8,128)}, u32[]{:S(2)}, u32[]{:S(2)}) %collective-permute-start.1) | collective-permute-done | bytes 131104 | tf_op jit(solution)/shard_map/while/body/eval_jaxpr/ppermute | solution.py:112
  (32 shorter events, 19.6 us)
Async XLA Ops:
  0.6 1.0 copy-start
  3.1 11.6 %collective-permute-start.2 = (f32[2,1,2,128,128]{3,4,2,0,1:T(8,128)S(1)}, f32[2,1,2,128,128]{3,4,2,0,1:T(8,128)S(1)}, u32[]{:S(2)}, u32[]{:S(2)}) collective-permute-start(f32[2,1,2,128,128]{3,4,2,0,1:T(8,128)S(1)} %bitcast.138), channel_id=1, source_target_pairs={{0,1},{1,2},{2,3},{3,0},{4,5},{5,6},{6,7},{7,4},{8,9},{9,10},{10,1... | collective-permute-start | bytes 786440 | tf_op jit(solution)/shard_map/ppermute | solution.py:24
  3.6 14.5 %collective-permute-start.4 = (f32[2,1,2,128,128]{3,4,2,0,1:T(8,128)S(1)}, f32[2,1,2,128,128]{3,4,2,0,1:T(8,128)S(1)}, u32[]{:S(2)}, u32[]{:S(2)}) collective-permute-start(f32[2,1,2,128,128]{3,4,2,0,1:T(8,128)S(1)} %bitcast.139), channel_id=1, source_target_pairs={{1,0},{2,1},{3,2},{0,3},{5,4},{6,5},{7,6},{4,7},{9,8},{10,9},{11,1... | collective-permute-start | bytes 786440 | tf_op jit(solution)/shard_map/ppermute | solution.py:27
  14.7 6.3 %collective-permute-start.3 = (f32[2,1,2,128,128]{3,4,2,0,1:T(8,128)S(1)}, f32[2,1,2,128,128]{3,4,2,0,1:T(8,128)S(1)}, u32[]{:S(2)}, u32[]{:S(2)}) collective-permute-start(f32[2,1,2,128,128]{3,4,2,0,1:T(8,128)S(1)} %collective-permute-done.2), channel_id=1, source_target_pairs={{0,1},{1,2},{2,3},{3,0},{4,5},{5,6},{6,7},{7,4},{8,9},{9,10},{10,1... | collective-permute-start | bytes 786440 | tf_op jit(solution)/shard_map/ppermute | solution.py:24
  33.6 6.5 %collective-permute-start = (f32[64,512]{1,0:T(8,128)}, f32[64,512]{1,0:T(8,128)S(1)}, u32[]{:S(2)}, u32[]{:S(2)}) collective-permute-start(f32[64,512]{1,0:T(8,128)} %convolution_add_fusion.7), channel_id=1, source_target_pairs={{0,4},{4,8},{8,12},{12,16},{16,20},{20,24},{24,28},{1,5},{5,9},{9,... | collective-permute-start | bytes 393224 | tf_op jit(solution)/shard_map/while/body/eval_jaxpr/ppermute | solution.py:98
  44.1 7.1 %collective-permute-start = (f32[64,512]{1,0:T(8,128)}, f32[64,512]{1,0:T(8,128)S(1)}, u32[]{:S(2)}, u32[]{:S(2)}) collective-permute-start(f32[64,512]{1,0:T(8,128)} %convolution_add_fusion.7), channel_id=1, source_target_pairs={{0,4},{4,8},{8,12},{12,16},{16,20},{20,24},{24,28},{1,5},{5,9},{9,... | collective-permute-start | bytes 393224 | tf_op jit(solution)/shard_map/while/body/eval_jaxpr/ppermute | solution.py:98
  55.1 7.2 %collective-permute-start = (f32[64,512]{1,0:T(8,128)}, f32[64,512]{1,0:T(8,128)S(1)}, u32[]{:S(2)}, u32[]{:S(2)}) collective-permute-start(f32[64,512]{1,0:T(8,128)} %convolution_add_fusion.7), channel_id=1, source_target_pairs={{0,4},{4,8},{8,12},{12,16},{16,20},{20,24},{24,28},{1,5},{5,9},{9,... | collective-permute-start | bytes 393224 | tf_op jit(solution)/shard_map/while/body/eval_jaxpr/ppermute | solution.py:98
  66.2 8.0 %collective-permute-start = (f32[64,512]{1,0:T(8,128)}, f32[64,512]{1,0:T(8,128)S(1)}, u32[]{:S(2)}, u32[]{:S(2)}) collective-permute-start(f32[64,512]{1,0:T(8,128)} %convolution_add_fusion.7), channel_id=1, source_target_pairs={{0,4},{4,8},{8,12},{12,16},{16,20},{20,24},{24,28},{1,5},{5,9},{9,... | collective-permute-start | bytes 393224 | tf_op jit(solution)/shard_map/while/body/eval_jaxpr/ppermute | solution.py:98
  78.1 8.0 %collective-permute-start = (f32[64,512]{1,0:T(8,128)}, f32[64,512]{1,0:T(8,128)S(1)}, u32[]{:S(2)}, u32[]{:S(2)}) collective-permute-start(f32[64,512]{1,0:T(8,128)} %convolution_add_fusion.7), channel_id=1, source_target_pairs={{0,4},{4,8},{8,12},{12,16},{16,20},{20,24},{24,28},{1,5},{5,9},{9,... | collective-permute-start | bytes 393224 | tf_op jit(solution)/shard_map/while/body/eval_jaxpr/ppermute | solution.py:98
  90.1 8.0 %collective-permute-start = (f32[64,512]{1,0:T(8,128)}, f32[64,512]{1,0:T(8,128)S(1)}, u32[]{:S(2)}, u32[]{:S(2)}) collective-permute-start(f32[64,512]{1,0:T(8,128)} %convolution_add_fusion.7), channel_id=1, source_target_pairs={{0,4},{4,8},{8,12},{12,16},{16,20},{20,24},{24,28},{1,5},{5,9},{9,... | collective-permute-start | bytes 393224 | tf_op jit(solution)/shard_map/while/body/eval_jaxpr/ppermute | solution.py:98
  102.0 8.0 %collective-permute-start = (f32[64,512]{1,0:T(8,128)}, f32[64,512]{1,0:T(8,128)S(1)}, u32[]{:S(2)}, u32[]{:S(2)}) collective-permute-start(f32[64,512]{1,0:T(8,128)} %convolution_add_fusion.7), channel_id=1, source_target_pairs={{0,4},{4,8},{8,12},{12,16},{16,20},{20,24},{24,28},{1,5},{5,9},{9,... | collective-permute-start | bytes 393224 | tf_op jit(solution)/shard_map/while/body/eval_jaxpr/ppermute | solution.py:98
  109.9 0.6 copy-start.1
  120.1 8.4 %collective-permute-start.1 = (f32[64,512]{1,0:T(8,128)}, f32[64,512]{1,0:T(8,128)}, u32[]{:S(2)}, u32[]{:S(2)}) collective-permute-start(f32[64,512]{1,0:T(8,128)} %fusion.67), channel_id=1, source_target_pairs={{4,0},{8,4},{12,8},{16,12},{20,16},{24,20},{28,24},{5,1},{9,5},{13... | collective-permute-start | bytes 393224 | tf_op jit(solution)/shard_map/while/body/eval_jaxpr/ppermute | solution.py:112
  132.4 9.7 %collective-permute-start.1 = (f32[64,512]{1,0:T(8,128)}, f32[64,512]{1,0:T(8,128)}, u32[]{:S(2)}, u32[]{:S(2)}) collective-permute-start(f32[64,512]{1,0:T(8,128)} %fusion.67), channel_id=1, source_target_pairs={{4,0},{8,4},{12,8},{16,12},{20,16},{24,20},{28,24},{5,1},{9,5},{13... | collective-permute-start | bytes 393224 | tf_op jit(solution)/shard_map/while/body/eval_jaxpr/ppermute | solution.py:112
  145.9 9.0 %collective-permute-start.1 = (f32[64,512]{1,0:T(8,128)}, f32[64,512]{1,0:T(8,128)}, u32[]{:S(2)}, u32[]{:S(2)}) collective-permute-start(f32[64,512]{1,0:T(8,128)} %fusion.67), channel_id=1, source_target_pairs={{4,0},{8,4},{12,8},{16,12},{20,16},{24,20},{28,24},{5,1},{9,5},{13... | collective-permute-start | bytes 393224 | tf_op jit(solution)/shard_map/while/body/eval_jaxpr/ppermute | solution.py:112
  158.8 7.8 %collective-permute-start.1 = (f32[64,512]{1,0:T(8,128)}, f32[64,512]{1,0:T(8,128)}, u32[]{:S(2)}, u32[]{:S(2)}) collective-permute-start(f32[64,512]{1,0:T(8,128)} %fusion.67), channel_id=1, source_target_pairs={{4,0},{8,4},{12,8},{16,12},{20,16},{24,20},{28,24},{5,1},{9,5},{13... | collective-permute-start | bytes 393224 | tf_op jit(solution)/shard_map/while/body/eval_jaxpr/ppermute | solution.py:112
  170.5 8.1 %collective-permute-start.1 = (f32[64,512]{1,0:T(8,128)}, f32[64,512]{1,0:T(8,128)}, u32[]{:S(2)}, u32[]{:S(2)}) collective-permute-start(f32[64,512]{1,0:T(8,128)} %fusion.67), channel_id=1, source_target_pairs={{4,0},{8,4},{12,8},{16,12},{20,16},{24,20},{28,24},{5,1},{9,5},{13... | collective-permute-start | bytes 393224 | tf_op jit(solution)/shard_map/while/body/eval_jaxpr/ppermute | solution.py:112
  182.4 8.1 %collective-permute-start.1 = (f32[64,512]{1,0:T(8,128)}, f32[64,512]{1,0:T(8,128)}, u32[]{:S(2)}, u32[]{:S(2)}) collective-permute-start(f32[64,512]{1,0:T(8,128)} %fusion.67), channel_id=1, source_target_pairs={{4,0},{8,4},{12,8},{16,12},{20,16},{24,20},{28,24},{5,1},{9,5},{13... | collective-permute-start | bytes 393224 | tf_op jit(solution)/shard_map/while/body/eval_jaxpr/ppermute | solution.py:112
  194.4 8.1 %collective-permute-start.1 = (f32[64,512]{1,0:T(8,128)}, f32[64,512]{1,0:T(8,128)}, u32[]{:S(2)}, u32[]{:S(2)}) collective-permute-start(f32[64,512]{1,0:T(8,128)} %fusion.67), channel_id=1, source_target_pairs={{4,0},{8,4},{12,8},{16,12},{20,16},{24,20},{28,24},{5,1},{9,5},{13... | collective-permute-start | bytes 393224 | tf_op jit(solution)/shard_map/while/body/eval_jaxpr/ppermute | solution.py:112
